TPU v7x, 512 devices: a whole 4x4x16 slice. The times are simulated.
512 devices in a mesh: dp: 16 (over z_hi, x), seq: 32 (over y, z_lo, core).
Axes of the slice: x: 4, y: 4, z: 16 (z_hi: 4, z_lo: 4; z = z_hi * 4 + z_lo), core: 2. Of those that a mesh axis runs over, the one named last changes fastest.
Arguments:
- binned_signals: bfloat16 [16, 16384, 768], P('dp', 'seq'), may hold values from -6 to 6
- kernel_coefficients: bfloat16 [5, 768, 768], P(None, 'dp'), may hold values from -0.09375 to 0.09375
- asking_projector: bfloat16 [768, 256], replicated, may hold values from -0.21875 to 0.21875
- lookup_projector: bfloat16 [768, 256], replicated, may hold values from -0.21875 to 0.21875
- content_projector: bfloat16 [768, 384], replicated, may hold values from -0.21875 to 0.21875
- readout_projector: bfloat16 [384, 768], replicated, may hold values from -0.3125 to 0.3125
- logit_multipliers: float32 [4], replicated, may hold values from 8 to 24
- loss_sensitivity: bfloat16 [16, 4096, 768], P('dp', 'seq'), may hold values from -0.0234375 to 0.0234375
Outputs:
- pooled: bfloat16 [16, 4096, 768], P('dp', 'seq')
- update: float32 [16, 4096, 768], P('dp', 'seq')
- query_grad: float32 [768, 256], replicated
- out_grad: float32 [384, 768], replicated
All inputs are finite; a program needn't handle non-finite values.
Results may differ from a plain program's by a relative error of at most 0.0095.
The roundings to bfloat16 on the way count: a program that leaves them out, or rounds other values in their place, can miss the bound.
Values may be sent and summed in bfloat16 or wider, within the bound.
No kernel may reach another device: no remote copies, remote signals or barrier semaphores. Data moves between devices by JAX's collectives and lax.ppermute only.
A program may use at most 128 MiB of HBM per device.

v0:
```python
import jax
import jax.numpy as jnp
from jax import lax
from jax.sharding import PartitionSpec as P

POOL = 4
norm_eps = 1e-05
head_eps = 1e-06


def padded_2(array, sides, width):
    for axis, dim in sides:
        devices, length = (lax.axis_size(axis), array.shape[dim])
        up = [(i, (i + 1) % devices) for i in range(devices - 1)]
        down = [(j, i) for i, j in up]
        last = lax.slice_in_dim(array, length - width, length, axis=dim)
        leading = lax.slice_in_dim(array, 0, width, axis=dim)
        before = lax.ppermute(last, axis, up)
        after = lax.ppermute(leading, axis, down)
        array = jnp.concatenate([before, array, after], axis=dim)
    return array


def layer_norm(values):
    centre = jnp.mean(values, axis=-1, keepdims=True)
    shifted = values - centre
    variance = jnp.mean(shifted * shifted, axis=-1, keepdims=True)
    return shifted * lax.rsqrt(variance + norm_eps)


def activate(values):
    return values * jax.nn.sigmoid(1.702 * values)


def head_norm(values, group_width):
    grouped = values.reshape(values.shape[0], -1, group_width)
    factor = lax.rsqrt(jnp.mean(grouped * grouped, axis=-1, keepdims=True) + head_eps)
    return (
        (grouped * factor).reshape(values.shape),
        jnp.broadcast_to(factor, grouped.shape).reshape(values.shape),
    )


def contract_first(former, latter):
    return lax.dot_general(
        former, latter, (((0,), (0,)), ((), ())), preferred_element_type=jnp.float32
    )


def contract_last(former, latter):
    return lax.dot_general(
        former, latter, (((1,), (1,)), ((), ())), preferred_element_type=jnp.float32
    )


def stacked_conv(padded, all_taps, length_fine):
    tap_count = all_taps.shape[0]
    windows = jnp.concatenate(
        [padded[tap_index : tap_index + length_fine] for tap_index in range(tap_count)], axis=1
    )
    flat_taps = all_taps.reshape(tap_count * all_taps.shape[1], all_taps.shape[2])
    return jnp.dot(windows, flat_taps, preferred_element_type=jnp.float32)


def on_device(
    binned_signals,
    kernel_coefficients,
    asking_projector,
    lookup_projector,
    content_projector,
    readout_projector,
    logit_multipliers,
    loss_sensitivity,
):
    incoming_tensor = binned_signals[0]
    directional_perturbations = loss_sensitivity[0]
    length_fine = incoming_tensor.shape[0]
    channels = incoming_tensor.shape[1]
    tap_count = kernel_coefficients.shape[0]
    margin = tap_count // 2
    attender_total = logit_multipliers.shape[0]
    probe_extent = asking_projector.shape[1] // attender_total
    value_width = content_projector.shape[1] // attender_total
    activated = activate(layer_norm(incoming_tensor.astype(jnp.float32))).astype(jnp.bfloat16)
    padded = padded_2(activated, (("seq", 0),), margin)
    all_taps = lax.all_gather(kernel_coefficients, "dp", axis=1, tiled=True)
    conv_sum = stacked_conv(padded, all_taps, length_fine)
    summed = incoming_tensor.astype(jnp.float32) + conv_sum
    pooled = jnp.max(summed.reshape(length_fine // POOL, POOL, channels), axis=1).astype(
        jnp.bfloat16
    )
    normed = layer_norm(pooled.astype(jnp.float32)).astype(jnp.bfloat16)
    queries = jnp.dot(normed, asking_projector, preferred_element_type=jnp.float32)
    query_hat, query_factor = head_norm(queries, probe_extent)
    query_unit = query_hat.astype(jnp.bfloat16)
    key_local = head_norm(
        jnp.dot(normed, lookup_projector, preferred_element_type=jnp.float32), probe_extent
    )[0].astype(jnp.bfloat16)
    value_local = jnp.dot(normed, content_projector, preferred_element_type=jnp.float32).astype(
        jnp.bfloat16
    )
    key_unit, values_all = (
        lax.all_gather(key_local, "seq", axis=0, tiled=True),
        lax.all_gather(value_local, "seq", axis=0, tiled=True),
    )
    heads_grad = contract_last(directional_perturbations, readout_projector).astype(jnp.bfloat16)
    outputs = []
    diffs = []
    for attender_slot in range(attender_total):
        key_lo = attender_slot * probe_extent
        value_lo = attender_slot * value_width
        query_part = query_unit[:, key_lo : key_lo + probe_extent]
        key_part = key_unit[:, key_lo : key_lo + probe_extent]
        value_part = values_all[:, value_lo : value_lo + value_width]
        attender_logit_gain = logit_multipliers[attender_slot] / probe_extent
        scores = contract_last(query_part, key_part) * attender_logit_gain
        expo = jnp.exp(scores)
        probs = expo / jnp.sum(expo, axis=1, keepdims=True)
        head_out = jnp.dot(
            probs.astype(jnp.bfloat16), value_part, preferred_element_type=jnp.float32
        )
        outputs.append(head_out)
        grad_part = heads_grad[:, value_lo : value_lo + value_width]
        prob_grad = contract_last(grad_part, value_part)
        delta = jnp.sum(grad_part.astype(jnp.float32) * head_out, axis=1, keepdims=True)
        score_grad = (probs * (prob_grad - delta)).astype(jnp.bfloat16)
        unit_grad = (
            jnp.dot(score_grad, key_part, preferred_element_type=jnp.float32) * attender_logit_gain
        )
        hat_part = query_hat[:, key_lo : key_lo + probe_extent]
        factor_part = query_factor[:, key_lo : key_lo + probe_extent]
        diffs.append(
            factor_part
            * (unit_grad - hat_part * jnp.mean(hat_part * unit_grad, axis=1, keepdims=True))
        )
    heads_low = jnp.concatenate(outputs, axis=1).astype(jnp.bfloat16)
    update = jnp.dot(heads_low, readout_projector, preferred_element_type=jnp.float32)
    query_diff = jnp.concatenate(diffs, axis=1).astype(jnp.bfloat16)
    query_local = contract_first(normed, query_diff)
    out_local = contract_first(heads_low, directional_perturbations)
    query_grad, out_grad = lax.psum((query_local, out_local), ("dp", "seq"))
    return (pooled[None], update[None], query_grad, out_grad)


def solution(mesh):
    return jax.shard_map(
        on_device,
        mesh=mesh,
        in_specs=(
            P("dp", "seq", None),
            P(None, "dp", None),
            P(),
            P(),
            P(),
            P(),
            P(),
            P("dp", "seq", None),
        ),
        out_specs=(P("dp", "seq", None), P("dp", "seq", None), P(), P()),
        check_vma=False,
    )
```

profile of v0, /device:TPU:2, one launch (start us, length us, event | category | flops | bytes accessed | tf_op | source)
XLA Modules:
  0.0 843.0 jit_solution(14659338999122518173)
XLA Ops:
  7.2 0.7 all-gather.4.cloned.1.call-update
  8.0 1.3 convert_reduce_fusion
  9.3 1.5 fusion.23
  10.8 0.6 fusion.22
  11.4 1.7 collective-permute-start
  13.2 1.3 collective-permute-start.1
  14.5 1.1 fusion.67
  15.6 1.1 fusion.69
  16.7 1.5 constant_dynamic-update-slice_fusion
  18.3 1.1 fusion.65
  19.4 1.2 fusion.68
  20.6 163.3 %all-gather.4.cloned.1.call-done = bf16[5,768,768]{2,1,0:T(8,128)(2,1)} async-done(((bf16[5,48,768]{2,1,0:T(8,128)(2,1)}), bf16[5,768,768]{2,1,0:T(8,128)(2,1)}) %all-gather.4.cloned.1.call-update) | async-done | bytes 5898256 | tf_op jit(solution)/shard_map/all_gather | solution.py:86
  183.9 7.1 fusion.12
  191.2 1.0 reduce_max.9
  192.4 0.2 fusion.72
  192.7 0.3 fusion.113
  193.2 0.6 multiply_convert_fusion
  193.9 1.0 convolution_convert_fusion.1
  194.9 0.2 all-reduce.3.cloned.1.call-start
  195.1 0.7 fusion.112
  198.4 0.3 convolution_convert_fusion
  198.7 0.3 fusion.114
  199.3 55.0 %all-gather.6.cloned.1.call-done = bf16[4096,256]{1,0:T(8,128)(2,1)} async-done(((bf16[128,256]{1,0:T(8,128)(2,1)}), bf16[4096,256]{1,0:T(8,128)(2,1)}) %all-gather.6.cloned.1.call-update) | async-done | bytes 2097168 | tf_op jit(solution)/shard_map/all_gather | solution.py:103
  254.3 3.3 fusion.118
  257.5 1.8 fusion.117
  259.4 1.9 fusion.116
  261.3 2.3 fusion.115
  263.7 58.5 %all-gather.8.cloned.1.call-done = bf16[4096,384]{1,0:T(8,128)(2,1)} async-done(((bf16[128,384]{1,0:T(8,128)(2,1)}), bf16[4096,384]{1,0:T(8,128)(2,1)}) %all-gather.8.cloned.1.call-update) | async-done | bytes 3145744 | tf_op jit(solution)/shard_map/all_gather | solution.py:104
  322.1 3.0 fusion.36
  325.2 0.4 copy-done.23
  325.6 1.0 fusion.38
  326.7 0.5 copy-done.5
  327.2 1.0 fusion.40
  328.2 0.5 copy-done.4
  328.8 1.1 multiply_reduce_fusion.7
  329.9 3.7 fusion.31
  333.7 3.9 fusion.30
  337.6 4.1 fusion.29
  341.6 4.0 multiply_reduce_fusion.3
  345.6 0.7 broadcast_multiply_fusion.3
  346.3 0.6 broadcast_multiply_fusion.1
  346.9 1.1 fusion.80
  348.1 1.3 fusion.81
  349.4 1.3 fusion.74
  350.7 1.0 convolution_bitcast_fusion
  351.7 481.5 %all-reduce.3.cloned.1.call-done = (f32[768,256]{1,0:T(8,128)}, f32[384,768]{1,0:T(8,128)}) async-done(((f32[768,256]{1,0:T(8,128)}, f32[384,768]{1,0:T(8,128)}), (f32[768,256]{1,0:T(8,128)}, f32[384,768]{1,0:T(8,128)})) %all-reduce.3.cloned.1.call-update) | async-done | bytes 1966096 | tf_op jit(solution)/shard_map/psum | solution.py:141
  833.3 2.2 copy.41
  835.4 1.0 copy.42
  (75 shorter events, 1.1 us)
Async XLA Ops:
  7.2 191.2 %copy-start = (bf16[384,768]{1,0:T(8,128)(2,1)S(1)}, bf16[384,768]{1,0:T(8,128)(2,1)}, u32[]{:S(2)}) copy-start(bf16[384,768]{1,0:T(8,128)(2,1)} %param.13) | copy-start | bytes 1769476
  7.2 3.6 copy-start.1
  7.2 176.7 %all-gather.4.cloned.1.call-start = ((), (), s32[]{:S(2)}) async-start(), calls=%async_computation | async-start | bytes 6266880 | tf_op jit(solution)/shard_map/all_gather | solution.py:86
  7.9 246.3 %all-gather.6.cloned.1.call-start = ((), (), s32[]{:S(2)}) async-start(), calls=%async_computation.1 | async-start | bytes 2162688 | tf_op jit(solution)/shard_map/all_gather | solution.py:103
  11.4 3.0 collective-permute-start
  13.2 5.1 collective-permute-start.1
  191.0 1.7 copy-start.9
  191.2 2.7 copy-start.24
  191.2 3.9 copy-start.13
  191.2 7.1 copy-start.8
  192.3 155.8 %copy-start.3 = (bf16[128,768]{1,0:T(8,128)(2,1)}, bf16[128,768]{1,0:T(8,128)(2,1)S(1)}, u32[]{:S(2)}) copy-start(bf16[128,768]{1,0:T(8,128)(2,1)S(1)} %reduce_max.9) | copy-start | bytes 589828
  192.4 6.3 copy-start.10
  192.4 6.5 copy-start.11
  192.6 6.3 copy-start.14
  193.9 128.3 %all-gather.8.cloned.1.call-start = ((), (), s32[]{:S(2)}) async-start(), calls=%async_computation.2 | async-start | bytes 3244032 | tf_op jit(solution)/shard_map/all_gather | solution.py:104
  194.9 638.4 %all-reduce.3.cloned.1.call-start = ((), (), s32[]{:S(2)}) async-start(), calls=%async_computation.3 | async-start | bytes 3932160 | tf_op jit(solution)/shard_map/psum | solution.py:141
  254.3 3.3 copy-start.2
  257.5 64.6 %copy-start.21 = (f32[128]{0:T(128)}, f32[128]{0:T(128)S(1)}, u32[]{:S(2)}) copy-start(f32[128]{0:T(128)S(1)} %get-tuple-element.40) | copy-start | bytes 1540
  259.4 65.8 %copy-start.19 = (f32[128]{0:T(128)}, f32[128]{0:T(128)S(1)}, u32[]{:S(2)}) copy-start(f32[128]{0:T(128)S(1)} %get-tuple-element.38) | copy-start | bytes 1540
  261.3 65.3 %copy-start.17 = (f32[128]{0:T(128)}, f32[128]{0:T(128)S(1)}, u32[]{:S(2)}) copy-start(f32[128]{0:T(128)S(1)} %get-tuple-element.36) | copy-start | bytes 1540
  322.1 3.0 copy-start.6
  322.1 3.5 copy-start.23
  325.6 1.6 copy-start.5
  327.2 1.6 copy-start.4
  327.2 1.6 copy-start.16
  328.8 1.1 copy-start.22
  329.9 3.7 copy-start.20
  333.7 3.9 copy-start.18
  333.7 3.9 copy-start.25
  341.6 6.5 copy-start.12
  341.6 6.5 copy-start.15
  833.3 2.2 copy-start.7
Sparse Core Ops, SparseCore 0:
  11.0 172.8 all-gather.3
  194.0 60.2 all-gather.5
  257.0 65.0 all-gather.7
  350.8 482.3 all-reduce.2
where the time goes:
time: 843 us
  waiting for transfers between devices  759 us (90%)
  matrix products  43.8 us (5%)
  between operations  16.7 us (2%)
  other arithmetic  14 us (2%)
    psum x1, waiting for transfers between devices, on_device(): query_grad, out_grad = lax.psum((query_local, out_local), ('dp', 'seq'))  482 us
    all_gather x1, waiting for transfers between devices, on_device(): all_taps = lax.all_gather(kernel_coefficients, 'dp', axis=1, tiled=True)  163 us
    all_gather x1, waiting for transfers between devices, on_device(): lax.all_gather(value_local, 'seq', axis=0, tiled=True)  58.5 us
    all_gather x1, waiting for transfers between devices, on_device(): lax.all_gather(key_local, 'seq', axis=0, tiled=True)  55 us
  transfers between devices with their start and end apart: 6, of which 4 were waited for; matrix products, arithmetic and copies ran while one was open for 3% of the time, Pallas kernels for 0%

commit v1 on v0

--- a/solution.py
+++ b/solution.py
@@ -101,7 +101,12 @@
     )
     key_unit, values_all = (
         lax.all_gather(key_local, "seq", axis=0, tiled=True),
-        lax.all_gather(value_local, "seq", axis=0, tiled=True),
+        jnp.concatenate(
+            lax.all_to_all(
+                jnp.stack([value_local for _ in range(lax.psum(1, "seq"))]), "seq", 0, 0
+            ),
+            axis=0,
+        ),
     )
     heads_grad = contract_last(directional_perturbations, readout_projector).astype(jnp.bfloat16)
     outputs = []

time: 843 us -> 815 us (0.967)
  waiting for transfers between devices: 759 us -> 721 us
    all_gather x1 -> x0, waiting for transfers between devices: 58.5 us -> none  [on_device(): lax.all_gather(value_local, 'seq', axis=0, tiled=True)]
    all_gather x1, waiting for transfers between devices: 55 us -> 77.9 us  [on_device(): lax.all_gather(key_local, 'seq', axis=0, tiled=True)]
  transfers between devices with their start and end apart: 6 -> 6, of which waited for: 4 -> 3; matrix products, arithmetic and copies ran while one was open for 3% -> 3% of each run, Pallas kernels for 0% -> 0%
where the time goes in v1:
time: 815 us
  waiting for transfers between devices  721 us (88%)
  matrix products  47.9 us (6%)
  between operations  16.7 us (2%)
  other arithmetic  14.1 us (2%)
  starting transfers between devices  8.27 us (1%)
    psum x1, waiting for transfers between devices, on_device(): query_grad, out_grad = lax.psum((query_local, out_local), ('dp', 'seq'))  479 us
    all_gather x1, waiting for transfers between devices, on_device(): all_taps = lax.all_gather(kernel_coefficients, 'dp', axis=1, tiled=True)  163 us
    all_gather x1, waiting for transfers between devices, on_device(): lax.all_gather(key_local, 'seq', axis=0, tiled=True)  77.9 us
  transfers between devices with their start and end apart: 6, of which 3 were waited for; matrix products, arithmetic and copies ran while one was open for 3% of the time, Pallas kernels for 0%

profile of v1, /device:TPU:2, one launch (start us, length us, event | category | flops | bytes accessed | tf_op | source)
XLA Modules:
  0.0 814.7 jit_solution(17917103347367748334)
XLA Ops:
  7.2 0.7 all-gather.3.cloned.1.call-update
  7.9 1.3 convert_reduce_fusion
  9.2 1.5 fusion.23
  10.8 0.6 fusion.22
  11.4 1.7 collective-permute-start
  13.1 1.3 collective-permute-start.1
  14.4 1.1 fusion.67
  15.6 1.1 fusion.69
  16.7 1.5 constant_dynamic-update-slice_fusion
  18.2 1.1 fusion.65
  19.3 1.2 fusion.68
  20.5 163.4 %all-gather.3.cloned.1.call-done = bf16[5,768,768]{2,1,0:T(8,128)(2,1)} async-done(((bf16[5,48,768]{2,1,0:T(8,128)(2,1)}), bf16[5,768,768]{2,1,0:T(8,128)(2,1)}) %all-gather.3.cloned.1.call-update) | async-done | bytes 5898256 | tf_op jit(solution)/shard_map/all_gather | solution.py:86
  183.9 7.1 fusion.12
  191.0 0.2 reshape.110
  191.2 1.0 reduce_max.9
  192.2 0.1 convert_reduce_fusion.1
  192.4 0.2 fusion.72
  192.6 0.3 convolution_convert_fusion.1
  192.9 2.2 stack.2
  195.1 4.9 all-to-all-start
  200.1 0.3 fusion.113
  200.7 0.6 multiply_convert_fusion
  201.3 0.2 all-reduce.3.cloned.1.call-start
  201.6 0.6 fusion.112
  204.7 0.3 convolution_convert_fusion
  205.0 0.3 fusion.114
  205.6 77.9 %all-gather.5.cloned.1.call-done = bf16[4096,256]{1,0:T(8,128)(2,1)} async-done(((bf16[128,256]{1,0:T(8,128)(2,1)}), bf16[4096,256]{1,0:T(8,128)(2,1)}) %all-gather.5.cloned.1.call-update) | async-done | bytes 2097168 | tf_op jit(solution)/shard_map/all_gather | solution.py:103
  283.5 3.3 fusion.116
  286.9 1.7 fusion.117
  288.6 1.9 fusion.118
  290.6 2.3 fusion.115
  292.9 3.4 fusion.40
  296.3 2.8 fusion.38
  299.1 2.4 fusion.36
  301.6 2.4 multiply_reduce_fusion.7
  304.0 3.8 fusion.31
  307.8 3.9 fusion.30
  311.6 4.1 fusion.29
  315.7 4.0 multiply_reduce_fusion.3
  319.7 0.7 broadcast_multiply_fusion.3
  320.4 0.7 broadcast_multiply_fusion.1
  321.1 1.1 fusion.80
  322.2 1.3 fusion.81
  323.5 1.3 fusion.74
  324.8 1.0 convolution_bitcast_fusion
  325.9 479.1 %all-reduce.3.cloned.1.call-done = (f32[768,256]{1,0:T(8,128)}, f32[384,768]{1,0:T(8,128)}) async-done(((f32[768,256]{1,0:T(8,128)}, f32[384,768]{1,0:T(8,128)}), (f32[768,256]{1,0:T(8,128)}, f32[384,768]{1,0:T(8,128)})) %all-reduce.3.cloned.1.call-update) | async-done | bytes 1966096 | tf_op jit(solution)/shard_map/psum | solution.py:146
  805.0 2.2 copy.41
  807.1 1.0 copy.42
  (73 shorter events, 0.7 us)
Async XLA Ops:
  7.2 197.5 %copy-start = (bf16[384,768]{1,0:T(8,128)(2,1)S(1)}, bf16[384,768]{1,0:T(8,128)(2,1)}, u32[]{:S(2)}) copy-start(bf16[384,768]{1,0:T(8,128)(2,1)} %param.13) | copy-start | bytes 1769476
  7.2 3.6 copy-start.1
  7.2 176.7 %all-gather.3.cloned.1.call-start = ((), (), s32[]{:S(2)}) async-start(), calls=%async_computation.1 | async-start | bytes 6266880 | tf_op jit(solution)/shard_map/all_gather | solution.py:86
  11.4 3.0 collective-permute-start
  13.1 5.1 collective-permute-start.1
  191.0 1.6 copy-start.23
  192.2 130.0 %copy-start.3 = (bf16[128,768]{1,0:T(8,128)(2,1)}, bf16[128,768]{1,0:T(8,128)(2,1)S(1)}, u32[]{:S(2)}) copy-start(bf16[128,768]{1,0:T(8,128)(2,1)S(1)} %reduce_max.9) | copy-start | bytes 589828
  192.4 12.6 %copy-start.11 = (f32[128]{0:T(128)}, f32[128]{0:T(128)S(1)}, u32[]{:S(2)}) copy-start(f32[128]{0:T(128)S(1)} %broadcast_multiply_fusion.5) | copy-start | bytes 1540
  192.6 12.4 %copy-start.14 = (f32[128]{0:T(128)}, f32[128]{0:T(128)S(1)}, u32[]{:S(2)}) copy-start(f32[128]{0:T(128)S(1)} %add_rsqrt_fusion.3) | copy-start | bytes 1540
  195.1 5.0 copy-start.9
  195.1 6.5 copy-start.13
  195.1 97.8 %all-to-all-start = ((bf16[32,128,384]{2,1,0:T(8,128)(2,1)}), bf16[32,128,384]{2,1,0:T(8,128)(2,1)}, u32[]{:S(2)}, u32[]{:S(2)}) async-start(bf16[32,128,384]{2,1,0:T(8,128)(2,1)} %stack.2), calls=%async_computation | async-start | bytes 6291456 | tf_op jit(solution)/shard_map/all_to_all | solution.py:105
  200.1 4.6 copy-start.8
  200.1 5.0 copy-start.10
  200.1 83.4 %all-gather.5.cloned.1.call-start = ((), (), s32[]{:S(2)}) async-start(), calls=%async_computation.2 | async-start | bytes 2162688 | tf_op jit(solution)/shard_map/all_gather | solution.py:103
  201.3 603.6 %all-reduce.3.cloned.1.call-start = ((), (), s32[]{:S(2)}) async-start(), calls=%async_computation.3 | async-start | bytes 3932160 | tf_op jit(solution)/shard_map/psum | solution.py:146
  283.5 3.4 copy-start.2
  286.9 6.0 copy-start.17
  288.6 7.7 copy-start.19
  290.6 8.5 %copy-start.21 = (f32[128]{0:T(128)}, f32[128]{0:T(128)S(1)}, u32[]{:S(2)}) copy-start(f32[128]{0:T(128)S(1)} %get-tuple-element.40) | copy-start | bytes 1540
  292.9 3.4 copy-start.5
  296.3 2.8 copy-start.6
  299.1 2.4 copy-start.4
  299.1 2.4 copy-start.16
  301.6 2.4 copy-start.22
  304.0 3.8 copy-start.20
  307.7 3.9 copy-start.18
  307.8 3.9 copy-start.24
  315.7 6.5 copy-start.12
  315.7 6.5 copy-start.15
  805.0 2.2 copy-start.7
Sparse Core Ops, SparseCore 0:
  11.0 172.8 all-gather.2
  203.6 79.8 all-gather.4
  325.0 479.9 all-reduce.2
